TPU v7x, 512 devices: a whole 4x8x8 slice. The times are simulated.
512 devices in a mesh: seq: 8 (over z_lo, core), ctx: 64 (over z_hi, y, x).
Axes of the slice: x: 4, y: 8, z: 8 (z_hi: 2, z_lo: 4; z = z_hi * 4 + z_lo), core: 2. Of those that a mesh axis runs over, the one named last changes fastest.
Arguments:
- tokens: bfloat16 [8, 8192, 2048], P('seq', 'ctx'), may hold values from -80 to 80
- qkv_weight: bfloat16 [2048, 1536], P(None, 'seq'), may hold values from -0.125 to 0.125
- doc_lengths: int32 [8, 36], P('seq'), may hold values from 1 to 1024, 8192 in all within a row
- span_order: int32 [8, 128], P('seq'), may hold values from 0 to 127, as said below
Outputs:
- attended: bfloat16 [8, 8192, 1024], P('seq', 'ctx')
Inputs may be any that keep to these rules, and one draw needn't show every extreme that they name: `doc_lengths`: each row sums to 8192; its largest entry is exactly 1024. `span_order`: in each row, slots 2 i and 2 i + 1 hold spans i and 127 - i, in an order drawn for each pair.
All inputs are finite; a program needn't handle non-finite values.
Results may differ from a plain program's by a relative error of at most 0.012.
The roundings to bfloat16 on the way count: a program that leaves them out, or rounds other values in their place, can miss the bound.
Values may be sent and summed in bfloat16 or wider, within the bound.
No kernel may reach another device: no remote copies, remote signals or barrier semaphores. Data moves between devices by JAX's collectives and lax.ppermute only.
A program may use at most 192 MiB of HBM per device.

v0:
```python
import jax
import jax.numpy as jnp
from jax import lax
from jax.sharding import PartitionSpec as P

QUERY_HEADS = 16
KEY_VALUE_HEADS = 4
HEAD_SIZE = 64
QUERY_PER_KV = 4
SPAN = 64


def shifted(value, axis, steps):
    count = lax.axis_size(axis)
    initial, last = (max(0, -steps), min(count, count - steps))
    return lax.ppermute(value, axis, [(source, source + steps) for source in range(initial, last)])


def apply_rotary(value_rows, token_positions):
    token_count = value_rows.shape[0]
    heads = value_rows.reshape(token_count, -1, HEAD_SIZE)
    half = HEAD_SIZE // 2
    freq = 500000.0 ** (-jnp.arange(half, dtype=jnp.float32) * 2.0 / HEAD_SIZE)
    angle = token_positions.astype(jnp.float32)[:, None] * freq[None, :]
    cosine = jnp.cos(angle)[:, None, :]
    sine = jnp.sin(angle)[:, None, :]
    first = heads[..., :half]
    second = heads[..., half:]
    turned = jnp.concatenate(
        [first * cosine - second * sine, second * cosine + first * sine], axis=-1
    )
    return turned.reshape(token_count, -1)


def positions(order_row):
    offsets = jnp.arange(SPAN, dtype=jnp.int32)
    return (order_row[:, None] * SPAN + offsets[None, :]).reshape(-1)


def documents(lengths_row, token_positions):
    ends = jnp.cumsum(lengths_row)
    return jnp.sum((ends[None, :] <= token_positions[:, None]).astype(jnp.int32), axis=1)


def body(tokens, qkv_weight, doc_lengths, span_order):
    rows = tokens[0]
    token_count = rows.shape[0]
    query_key_value = jnp.dot(
        rows,
        lax.all_gather(qkv_weight, "seq", axis=1, tiled=True),
        preferred_element_type=jnp.float32,
    ).astype(jnp.bfloat16)
    lengths_row = doc_lengths[0]
    order_row = span_order[0]
    places_all = positions(order_row)
    docs_all = documents(lengths_row, places_all)
    my_index = lax.axis_index("ctx")
    first_row = my_index * token_count
    token_positions = lax.dynamic_slice_in_dim(places_all, first_row, token_count)
    docs = lax.dynamic_slice_in_dim(docs_all, first_row, token_count)
    query_rows = apply_rotary(
        query_key_value[:, : QUERY_HEADS * HEAD_SIZE].astype(jnp.float32), token_positions
    ).astype(jnp.bfloat16)
    key_rows = apply_rotary(
        query_key_value[
            :, QUERY_HEADS * HEAD_SIZE : (QUERY_HEADS + KEY_VALUE_HEADS) * HEAD_SIZE
        ].astype(jnp.float32),
        token_positions,
    ).astype(jnp.bfloat16)
    value_rows = query_key_value[:, (QUERY_HEADS + KEY_VALUE_HEADS) * HEAD_SIZE :]
    query_head_rows = query_rows.reshape(token_count, KEY_VALUE_HEADS, QUERY_PER_KV, HEAD_SIZE)

    def absorb_block(carry, key_block_part, value_block_part, key_places, key_docs, usable):
        block_rows = key_block_part.shape[0]
        live = (
            (docs[:, None] == key_docs[None, :])
            & (key_places[None, :] <= token_positions[:, None])
            & usable
        )
        running_state, total, summed = carry
        key_head_rows = key_block_part.reshape(block_rows, KEY_VALUE_HEADS, HEAD_SIZE)
        value_head_rows = value_block_part.reshape(block_rows, KEY_VALUE_HEADS, HEAD_SIZE)
        scores = (
            jnp.einsum(
                "qhgd,khd->hgqk", query_head_rows, key_head_rows, preferred_element_type=jnp.float32
            )
            * 0.125
        )
        scores = jnp.where(live, scores, -1e30)
        newest = jnp.maximum(running_state, jnp.max(scores, axis=-1))
        factor = jnp.exp(running_state - newest)
        weights = jnp.where(live, jnp.exp(scores - newest[..., None]), 0.0)
        total = total * factor + jnp.sum(weights, axis=-1)
        added = jnp.einsum(
            "hgqk,khd->hgqd",
            weights.astype(jnp.bfloat16),
            value_head_rows,
            preferred_element_type=jnp.float32,
        )
        summed = summed * factor[..., None] + added
        return (newest, total, summed)

    initial = (
        jnp.full((KEY_VALUE_HEADS, QUERY_PER_KV, token_count), -1e30, jnp.float32),
        jnp.zeros((KEY_VALUE_HEADS, QUERY_PER_KV, token_count), jnp.float32),
        jnp.zeros((KEY_VALUE_HEADS, QUERY_PER_KV, token_count, HEAD_SIZE), jnp.float32),
    )
    devices = lax.axis_size("ctx")
    key_cols = key_rows.shape[1]
    stacked = jnp.concatenate([key_rows, value_rows], axis=1)
    early_first = order_row[2 * my_index] < devices
    offset = jnp.where(early_first, 0, SPAN).astype(jnp.int32)
    early_rows = lax.dynamic_slice_in_dim(stacked, offset, SPAN, 0)
    late_rows = lax.dynamic_slice_in_dim(stacked, SPAN - offset, SPAN, 0)
    pair_rows = jnp.concatenate([early_rows, late_rows], axis=0)
    ramp = jnp.arange(SPAN, dtype=jnp.int32)
    state = absorb_block(initial, key_rows, value_rows, token_positions, docs, jnp.array(True))

    def advance(step, loop_state):
        carry, upward, downward = loop_state
        upward = shifted(upward, "ctx", 1)
        downward = shifted(downward, "ctx", -1)
        lower = my_index - step
        upper = my_index + step
        up_places = lower * SPAN + ramp
        carry = absorb_block(
            carry,
            upward[:, :key_cols],
            upward[:, key_cols:],
            up_places,
            documents(lengths_row, up_places),
            lower >= 0,
        )
        down_places = jnp.concatenate(
            [upper * SPAN + ramp, (2 * devices - 1 - upper) * SPAN + ramp]
        )
        carry = absorb_block(
            carry,
            downward[:, :key_cols],
            downward[:, key_cols:],
            down_places,
            documents(lengths_row, down_places),
            upper < devices,
        )
        return (carry, upward, downward)

    final_state = lax.fori_loop(1, devices // 4 + 1, advance, (state, early_rows, pair_rows))
    running_state, total, summed = final_state[0]
    outputs = summed / total[..., None]
    outputs = (
        jnp.transpose(outputs, (2, 0, 1, 3))
        .reshape(token_count, QUERY_HEADS * HEAD_SIZE)
        .astype(jnp.bfloat16)
    )
    return outputs[None]


def solution(mesh):
    placed = (P("seq", "ctx", None), P(None, "seq"), P("seq", None), P("seq", None))
    return jax.shard_map(
        body, mesh=mesh, in_specs=placed, out_specs=P("seq", "ctx", None), check_vma=False
    )
```

profile of v0, /device:TPU:448, one launch (start us, length us, event | category | flops | bytes accessed | tf_op | source)
XLA Modules:
  0.0 397.3 jit_solution(10987647458740105769)
XLA Ops:
  12.5 69.8 %all-gather.2.cloned.1.call-done = bf16[2048,1536]{0,1:T(8,128)(2,1)} async-done(((bf16[2048,192]{0,1:T(8,128)(2,1)}), bf16[2048,1536]{0,1:T(8,128)(2,1)}) %all-gather.2.cloned.1.call-update) | async-done | bytes 6291472 | tf_op jit(solution)/shard_map/all_gather | solution.py:50
  82.3 5.0 %convolution_convert_fusion = bf16[128,1536]{1,0:T(8,128)(2,1)S(1)} fusion(bf16[2048,1536]{0,1:T(8,128)(2,1)} %all-gather.2.cloned.1.call-done, bf16[1,128,2048]{2,1,0:T(8,128)(2,1)S(1)} %copy-done), kind=kOutput, calls=%fused_computation.36 | convolution fusion | flops 805502976 | bytes 7208960 | tf_op jit(solution)/shard_map/dot_general | solution.py:48
  89.2 300.4 %while.25 = (s32[]{:T(128)}, f32[4,4,128]{2,1,0:T(4,128)S(1)}, f32[4,4,128]{2,1,0:T(4,128)S(1)}, f32[4,4,128,64]{2,3,1,0:T(8,128)S(1)}, bf16[64,512]{1,0:T(8,128...) while((s32[]{:T(128)}, f32[4,4,128]{2,1,0:T(4,128)S(1)}, ...), condition=%wide.region_12.13_spmd.clone.clone, body=%wide.region_5.12_spmd.clone.clone.sunk | while | flops 104853896 | bytes 9559397 | solution.py:147
  89.2 9.7 %collective-permute-start = (bf16[128,512]{0,1:T(8,128)(2,1)S(1)}, bf16[128,512]{0,1:T(8,128)(2,1)S(1)}, u32[]{:S(2)}, u32[]{:S(2)}) collective-permute-start(bf16[128,512]{0,1:T(8,128)(2,1)S(1)} %get-tuple-element.555), channel_id=1, source_target_pairs={{1,0},{2,1},{3,2},{4,3},{5,4},{6,5},{7,6},{8,7},{9,8},{10,9},{11,1... | collective-permute-start | bytes 393224 | tf_op jit(solution)/shard_map/while/body/eval_jaxpr/ppermute | solution.py:16
  101.3 11.9 %collective-permute-done.1 = bf16[64,512]{1,0:T(8,128)(2,1)S(1)} collective-permute-done((bf16[64,512]{1,0:T(8,128)(2,1)S(1)}, bf16[64,512]{1,0:T(8,128)(2,1)S(1)}, u32[]{:S(2)}, u32[]{:S(2)}) %collective-permute-start.1) | collective-permute-done | bytes 65568 | tf_op jit(solution)/shard_map/while/body/eval_jaxpr/ppermute | solution.py:16
  116.9 3.9 collective-permute-start.1
  121.4 9.9 %collective-permute-done.1 = bf16[64,512]{1,0:T(8,128)(2,1)S(1)} collective-permute-done((bf16[64,512]{1,0:T(8,128)(2,1)S(1)}, bf16[64,512]{1,0:T(8,128)(2,1)S(1)}, u32[]{:S(2)}, u32[]{:S(2)}) %collective-permute-start.1) | collective-permute-done | bytes 65568 | tf_op jit(solution)/shard_map/while/body/eval_jaxpr/ppermute | solution.py:16
  139.4 10.4 %collective-permute-done.1 = bf16[64,512]{1,0:T(8,128)(2,1)S(1)} collective-permute-done((bf16[64,512]{1,0:T(8,128)(2,1)S(1)}, bf16[64,512]{1,0:T(8,128)(2,1)S(1)}, u32[]{:S(2)}, u32[]{:S(2)}) %collective-permute-start.1) | collective-permute-done | bytes 65568 | tf_op jit(solution)/shard_map/while/body/eval_jaxpr/ppermute | solution.py:16
  153.6 3.9 collective-permute-start.1
  158.0 10.0 %collective-permute-done.1 = bf16[64,512]{1,0:T(8,128)(2,1)S(1)} collective-permute-done((bf16[64,512]{1,0:T(8,128)(2,1)S(1)}, bf16[64,512]{1,0:T(8,128)(2,1)S(1)}, u32[]{:S(2)}, u32[]{:S(2)}) %collective-permute-start.1) | collective-permute-done | bytes 65568 | tf_op jit(solution)/shard_map/while/body/eval_jaxpr/ppermute | solution.py:16
  176.2 10.0 %collective-permute-done.1 = bf16[64,512]{1,0:T(8,128)(2,1)S(1)} collective-permute-done((bf16[64,512]{1,0:T(8,128)(2,1)S(1)}, bf16[64,512]{1,0:T(8,128)(2,1)S(1)}, u32[]{:S(2)}, u32[]{:S(2)}) %collective-permute-start.1) | collective-permute-done | bytes 65568 | tf_op jit(solution)/shard_map/while/body/eval_jaxpr/ppermute | solution.py:16
  194.3 10.0 %collective-permute-done.1 = bf16[64,512]{1,0:T(8,128)(2,1)S(1)} collective-permute-done((bf16[64,512]{1,0:T(8,128)(2,1)S(1)}, bf16[64,512]{1,0:T(8,128)(2,1)S(1)}, u32[]{:S(2)}, u32[]{:S(2)}) %collective-permute-start.1) | collective-permute-done | bytes 65568 | tf_op jit(solution)/shard_map/while/body/eval_jaxpr/ppermute | solution.py:16
  212.5 10.0 %collective-permute-done.1 = bf16[64,512]{1,0:T(8,128)(2,1)S(1)} collective-permute-done((bf16[64,512]{1,0:T(8,128)(2,1)S(1)}, bf16[64,512]{1,0:T(8,128)(2,1)S(1)}, u32[]{:S(2)}, u32[]{:S(2)}) %collective-permute-start.1) | collective-permute-done | bytes 65568 | tf_op jit(solution)/shard_map/while/body/eval_jaxpr/ppermute | solution.py:16
  230.7 10.0 %collective-permute-done.1 = bf16[64,512]{1,0:T(8,128)(2,1)S(1)} collective-permute-done((bf16[64,512]{1,0:T(8,128)(2,1)S(1)}, bf16[64,512]{1,0:T(8,128)(2,1)S(1)}, u32[]{:S(2)}, u32[]{:S(2)}) %collective-permute-start.1) | collective-permute-done | bytes 65568 | tf_op jit(solution)/shard_map/while/body/eval_jaxpr/ppermute | solution.py:16
  244.4 3.9 collective-permute-start.1
  248.9 10.0 %collective-permute-done.1 = bf16[64,512]{1,0:T(8,128)(2,1)S(1)} collective-permute-done((bf16[64,512]{1,0:T(8,128)(2,1)S(1)}, bf16[64,512]{1,0:T(8,128)(2,1)S(1)}, u32[]{:S(2)}, u32[]{:S(2)}) %collective-permute-start.1) | collective-permute-done | bytes 65568 | tf_op jit(solution)/shard_map/while/body/eval_jaxpr/ppermute | solution.py:16
  267.0 10.0 %collective-permute-done.1 = bf16[64,512]{1,0:T(8,128)(2,1)S(1)} collective-permute-done((bf16[64,512]{1,0:T(8,128)(2,1)S(1)}, bf16[64,512]{1,0:T(8,128)(2,1)S(1)}, u32[]{:S(2)}, u32[]{:S(2)}) %collective-permute-start.1) | collective-permute-done | bytes 65568 | tf_op jit(solution)/shard_map/while/body/eval_jaxpr/ppermute | solution.py:16
  285.2 10.0 %collective-permute-done.1 = bf16[64,512]{1,0:T(8,128)(2,1)S(1)} collective-permute-done((bf16[64,512]{1,0:T(8,128)(2,1)S(1)}, bf16[64,512]{1,0:T(8,128)(2,1)S(1)}, u32[]{:S(2)}, u32[]{:S(2)}) %collective-permute-start.1) | collective-permute-done | bytes 65568 | tf_op jit(solution)/shard_map/while/body/eval_jaxpr/ppermute | solution.py:16
  303.4 10.0 %collective-permute-done.1 = bf16[64,512]{1,0:T(8,128)(2,1)S(1)} collective-permute-done((bf16[64,512]{1,0:T(8,128)(2,1)S(1)}, bf16[64,512]{1,0:T(8,128)(2,1)S(1)}, u32[]{:S(2)}, u32[]{:S(2)}) %collective-permute-start.1) | collective-permute-done | bytes 65568 | tf_op jit(solution)/shard_map/while/body/eval_jaxpr/ppermute | solution.py:16
  321.6 10.0 %collective-permute-done.1 = bf16[64,512]{1,0:T(8,128)(2,1)S(1)} collective-permute-done((bf16[64,512]{1,0:T(8,128)(2,1)S(1)}, bf16[64,512]{1,0:T(8,128)(2,1)S(1)}, u32[]{:S(2)}, u32[]{:S(2)}) %collective-permute-start.1) | collective-permute-done | bytes 65568 | tf_op jit(solution)/shard_map/while/body/eval_jaxpr/ppermute | solution.py:16
  335.3 3.9 collective-permute-start.1
  339.7 11.2 %collective-permute-done.1 = bf16[64,512]{1,0:T(8,128)(2,1)S(1)} collective-permute-done((bf16[64,512]{1,0:T(8,128)(2,1)S(1)}, bf16[64,512]{1,0:T(8,128)(2,1)S(1)}, u32[]{:S(2)}, u32[]{:S(2)}) %collective-permute-start.1) | collective-permute-done | bytes 65568 | tf_op jit(solution)/shard_map/while/body/eval_jaxpr/ppermute | solution.py:16
  359.2 10.1 %collective-permute-done.1 = bf16[64,512]{1,0:T(8,128)(2,1)S(1)} collective-permute-done((bf16[64,512]{1,0:T(8,128)(2,1)S(1)}, bf16[64,512]{1,0:T(8,128)(2,1)S(1)}, u32[]{:S(2)}, u32[]{:S(2)}) %collective-permute-start.1) | collective-permute-done | bytes 65568 | tf_op jit(solution)/shard_map/while/body/eval_jaxpr/ppermute | solution.py:16
  377.5 10.2 %collective-permute-done.1 = bf16[64,512]{1,0:T(8,128)(2,1)S(1)} collective-permute-done((bf16[64,512]{1,0:T(8,128)(2,1)S(1)}, bf16[64,512]{1,0:T(8,128)(2,1)S(1)}, u32[]{:S(2)}, u32[]{:S(2)}) %collective-permute-start.1) | collective-permute-done | bytes 65568 | tf_op jit(solution)/shard_map/while/body/eval_jaxpr/ppermute | solution.py:16
  (433 shorter events, 116.8 us)
Async XLA Ops:
  6.5 75.8 %all-gather.2.cloned.1.call-start = ((), (), s32[]{:S(2)}) async-start(), calls=%async_computation | async-start | bytes 7077888 | tf_op jit(solution)/shard_map/all_gather | solution.py:50
  89.2 24.5 %collective-permute-start = (bf16[128,512]{0,1:T(8,128)(2,1)S(1)}, bf16[128,512]{0,1:T(8,128)(2,1)S(1)}, u32[]{:S(2)}, u32[]{:S(2)}) collective-permute-start(bf16[128,512]{0,1:T(8,128)(2,1)S(1)} %get-tuple-element.555), channel_id=1, source_target_pairs={{1,0},{2,1},{3,2},{4,3},{5,4},{6,5},{7,6},{8,7},{9,8},{10,9},{11,1... | collective-permute-start | bytes 393224 | tf_op jit(solution)/shard_map/while/body/eval_jaxpr/ppermute | solution.py:16
  115.0 16.7 %collective-permute-start = (bf16[128,512]{0,1:T(8,128)(2,1)S(1)}, bf16[128,512]{0,1:T(8,128)(2,1)S(1)}, u32[]{:S(2)}, u32[]{:S(2)}) collective-permute-start(bf16[128,512]{0,1:T(8,128)(2,1)S(1)} %get-tuple-element.555), channel_id=1, source_target_pairs={{1,0},{2,1},{3,2},{4,3},{5,4},{6,5},{7,6},{8,7},{9,8},{10,9},{11,1... | collective-permute-start | bytes 393224 | tf_op jit(solution)/shard_map/while/body/eval_jaxpr/ppermute | solution.py:16
  133.0 17.3 %collective-permute-start = (bf16[128,512]{0,1:T(8,128)(2,1)S(1)}, bf16[128,512]{0,1:T(8,128)(2,1)S(1)}, u32[]{:S(2)}, u32[]{:S(2)}) collective-permute-start(bf16[128,512]{0,1:T(8,128)(2,1)S(1)} %get-tuple-element.555), channel_id=1, source_target_pairs={{1,0},{2,1},{3,2},{4,3},{5,4},{6,5},{7,6},{8,7},{9,8},{10,9},{11,1... | collective-permute-start | bytes 393224 | tf_op jit(solution)/shard_map/while/body/eval_jaxpr/ppermute | solution.py:16
  135.4 14.4 %collective-permute-start.1 = (bf16[64,512]{1,0:T(8,128)(2,1)S(1)}, bf16[64,512]{1,0:T(8,128)(2,1)S(1)}, u32[]{:S(2)}, u32[]{:S(2)}) collective-permute-start(bf16[64,512]{1,0:T(8,128)(2,1)S(1)} %get-tuple-element.554), channel_id=1, source_target_pairs={{0,1},{1,2},{2,3},{3,4},{4,5},{5,6},{6,7},{7,8},{8,9},{9,10},{10,1... | collective-permute-start | bytes 196616 | tf_op jit(solution)/shard_map/while/body/eval_jaxpr/ppermute | solution.py:16
  151.7 16.8 %collective-permute-start = (bf16[128,512]{0,1:T(8,128)(2,1)S(1)}, bf16[128,512]{0,1:T(8,128)(2,1)S(1)}, u32[]{:S(2)}, u32[]{:S(2)}) collective-permute-start(bf16[128,512]{0,1:T(8,128)(2,1)S(1)} %get-tuple-element.555), channel_id=1, source_target_pairs={{1,0},{2,1},{3,2},{4,3},{5,4},{6,5},{7,6},{8,7},{9,8},{10,9},{11,1... | collective-permute-start | bytes 393224 | tf_op jit(solution)/shard_map/while/body/eval_jaxpr/ppermute | solution.py:16
  153.6 14.4 %collective-permute-start.1 = (bf16[64,512]{1,0:T(8,128)(2,1)S(1)}, bf16[64,512]{1,0:T(8,128)(2,1)S(1)}, u32[]{:S(2)}, u32[]{:S(2)}) collective-permute-start(bf16[64,512]{1,0:T(8,128)(2,1)S(1)} %get-tuple-element.554), channel_id=1, source_target_pairs={{0,1},{1,2},{2,3},{3,4},{4,5},{5,6},{6,7},{7,8},{8,9},{9,10},{10,1... | collective-permute-start | bytes 196616 | tf_op jit(solution)/shard_map/while/body/eval_jaxpr/ppermute | solution.py:16
  169.8 16.8 %collective-permute-start = (bf16[128,512]{0,1:T(8,128)(2,1)S(1)}, bf16[128,512]{0,1:T(8,128)(2,1)S(1)}, u32[]{:S(2)}, u32[]{:S(2)}) collective-permute-start(bf16[128,512]{0,1:T(8,128)(2,1)S(1)} %get-tuple-element.555), channel_id=1, source_target_pairs={{1,0},{2,1},{3,2},{4,3},{5,4},{6,5},{7,6},{8,7},{9,8},{10,9},{11,1... | collective-permute-start | bytes 393224 | tf_op jit(solution)/shard_map/while/body/eval_jaxpr/ppermute | solution.py:16
  188.0 16.8 %collective-permute-start = (bf16[128,512]{0,1:T(8,128)(2,1)S(1)}, bf16[128,512]{0,1:T(8,128)(2,1)S(1)}, u32[]{:S(2)}, u32[]{:S(2)}) collective-permute-start(bf16[128,512]{0,1:T(8,128)(2,1)S(1)} %get-tuple-element.555), channel_id=1, source_target_pairs={{1,0},{2,1},{3,2},{4,3},{5,4},{6,5},{7,6},{8,7},{9,8},{10,9},{11,1... | collective-permute-start | bytes 393224 | tf_op jit(solution)/shard_map/while/body/eval_jaxpr/ppermute | solution.py:16
  206.2 16.8 %collective-permute-start = (bf16[128,512]{0,1:T(8,128)(2,1)S(1)}, bf16[128,512]{0,1:T(8,128)(2,1)S(1)}, u32[]{:S(2)}, u32[]{:S(2)}) collective-permute-start(bf16[128,512]{0,1:T(8,128)(2,1)S(1)} %get-tuple-element.555), channel_id=1, source_target_pairs={{1,0},{2,1},{3,2},{4,3},{5,4},{6,5},{7,6},{8,7},{9,8},{10,9},{11,1... | collective-permute-start | bytes 393224 | tf_op jit(solution)/shard_map/while/body/eval_jaxpr/ppermute | solution.py:16
  208.1 14.4 %collective-permute-start.1 = (bf16[64,512]{1,0:T(8,128)(2,1)S(1)}, bf16[64,512]{1,0:T(8,128)(2,1)S(1)}, u32[]{:S(2)}, u32[]{:S(2)}) collective-permute-start(bf16[64,512]{1,0:T(8,128)(2,1)S(1)} %get-tuple-element.554), channel_id=1, source_target_pairs={{0,1},{1,2},{2,3},{3,4},{4,5},{5,6},{6,7},{7,8},{8,9},{9,10},{10,1... | collective-permute-start | bytes 196616 | tf_op jit(solution)/shard_map/while/body/eval_jaxpr/ppermute | solution.py:16
  224.3 16.8 %collective-permute-start = (bf16[128,512]{0,1:T(8,128)(2,1)S(1)}, bf16[128,512]{0,1:T(8,128)(2,1)S(1)}, u32[]{:S(2)}, u32[]{:S(2)}) collective-permute-start(bf16[128,512]{0,1:T(8,128)(2,1)S(1)} %get-tuple-element.555), channel_id=1, source_target_pairs={{1,0},{2,1},{3,2},{4,3},{5,4},{6,5},{7,6},{8,7},{9,8},{10,9},{11,1... | collective-permute-start | bytes 393224 | tf_op jit(solution)/shard_map/while/body/eval_jaxpr/ppermute | solution.py:16
  242.5 16.8 %collective-permute-start = (bf16[128,512]{0,1:T(8,128)(2,1)S(1)}, bf16[128,512]{0,1:T(8,128)(2,1)S(1)}, u32[]{:S(2)}, u32[]{:S(2)}) collective-permute-start(bf16[128,512]{0,1:T(8,128)(2,1)S(1)} %get-tuple-element.555), channel_id=1, source_target_pairs={{1,0},{2,1},{3,2},{4,3},{5,4},{6,5},{7,6},{8,7},{9,8},{10,9},{11,1... | collective-permute-start | bytes 393224 | tf_op jit(solution)/shard_map/while/body/eval_jaxpr/ppermute | solution.py:16
  244.4 14.4 %collective-permute-start.1 = (bf16[64,512]{1,0:T(8,128)(2,1)S(1)}, bf16[64,512]{1,0:T(8,128)(2,1)S(1)}, u32[]{:S(2)}, u32[]{:S(2)}) collective-permute-start(bf16[64,512]{1,0:T(8,128)(2,1)S(1)} %get-tuple-element.554), channel_id=1, source_target_pairs={{0,1},{1,2},{2,3},{3,4},{4,5},{5,6},{6,7},{7,8},{8,9},{9,10},{10,1... | collective-permute-start | bytes 196616 | tf_op jit(solution)/shard_map/while/body/eval_jaxpr/ppermute | solution.py:16
  260.7 16.8 %collective-permute-start = (bf16[128,512]{0,1:T(8,128)(2,1)S(1)}, bf16[128,512]{0,1:T(8,128)(2,1)S(1)}, u32[]{:S(2)}, u32[]{:S(2)}) collective-permute-start(bf16[128,512]{0,1:T(8,128)(2,1)S(1)} %get-tuple-element.555), channel_id=1, source_target_pairs={{1,0},{2,1},{3,2},{4,3},{5,4},{6,5},{7,6},{8,7},{9,8},{10,9},{11,1... | collective-permute-start | bytes 393224 | tf_op jit(solution)/shard_map/while/body/eval_jaxpr/ppermute | solution.py:16
  278.9 16.8 %collective-permute-start = (bf16[128,512]{0,1:T(8,128)(2,1)S(1)}, bf16[128,512]{0,1:T(8,128)(2,1)S(1)}, u32[]{:S(2)}, u32[]{:S(2)}) collective-permute-start(bf16[128,512]{0,1:T(8,128)(2,1)S(1)} %get-tuple-element.555), channel_id=1, source_target_pairs={{1,0},{2,1},{3,2},{4,3},{5,4},{6,5},{7,6},{8,7},{9,8},{10,9},{11,1... | collective-permute-start | bytes 393224 | tf_op jit(solution)/shard_map/while/body/eval_jaxpr/ppermute | solution.py:16
  297.0 16.8 %collective-permute-start = (bf16[128,512]{0,1:T(8,128)(2,1)S(1)}, bf16[128,512]{0,1:T(8,128)(2,1)S(1)}, u32[]{:S(2)}, u32[]{:S(2)}) collective-permute-start(bf16[128,512]{0,1:T(8,128)(2,1)S(1)} %get-tuple-element.555), channel_id=1, source_target_pairs={{1,0},{2,1},{3,2},{4,3},{5,4},{6,5},{7,6},{8,7},{9,8},{10,9},{11,1... | collective-permute-start | bytes 393224 | tf_op jit(solution)/shard_map/while/body/eval_jaxpr/ppermute | solution.py:16
  299.0 14.4 %collective-permute-start.1 = (bf16[64,512]{1,0:T(8,128)(2,1)S(1)}, bf16[64,512]{1,0:T(8,128)(2,1)S(1)}, u32[]{:S(2)}, u32[]{:S(2)}) collective-permute-start(bf16[64,512]{1,0:T(8,128)(2,1)S(1)} %get-tuple-element.554), channel_id=1, source_target_pairs={{0,1},{1,2},{2,3},{3,4},{4,5},{5,6},{6,7},{7,8},{8,9},{9,10},{10,1... | collective-permute-start | bytes 196616 | tf_op jit(solution)/shard_map/while/body/eval_jaxpr/ppermute | solution.py:16
  315.2 16.8 %collective-permute-start = (bf16[128,512]{0,1:T(8,128)(2,1)S(1)}, bf16[128,512]{0,1:T(8,128)(2,1)S(1)}, u32[]{:S(2)}, u32[]{:S(2)}) collective-permute-start(bf16[128,512]{0,1:T(8,128)(2,1)S(1)} %get-tuple-element.555), channel_id=1, source_target_pairs={{1,0},{2,1},{3,2},{4,3},{5,4},{6,5},{7,6},{8,7},{9,8},{10,9},{11,1... | collective-permute-start | bytes 393224 | tf_op jit(solution)/shard_map/while/body/eval_jaxpr/ppermute | solution.py:16
  333.4 18.1 %collective-permute-start = (bf16[128,512]{0,1:T(8,128)(2,1)S(1)}, bf16[128,512]{0,1:T(8,128)(2,1)S(1)}, u32[]{:S(2)}, u32[]{:S(2)}) collective-permute-start(bf16[128,512]{0,1:T(8,128)(2,1)S(1)} %get-tuple-element.555), channel_id=1, source_target_pairs={{1,0},{2,1},{3,2},{4,3},{5,4},{6,5},{7,6},{8,7},{9,8},{10,9},{11,1... | collective-permute-start | bytes 393224 | tf_op jit(solution)/shard_map/while/body/eval_jaxpr/ppermute | solution.py:16
  335.3 15.7 %collective-permute-start.1 = (bf16[64,512]{1,0:T(8,128)(2,1)S(1)}, bf16[64,512]{1,0:T(8,128)(2,1)S(1)}, u32[]{:S(2)}, u32[]{:S(2)}) collective-permute-start(bf16[64,512]{1,0:T(8,128)(2,1)S(1)} %get-tuple-element.554), channel_id=1, source_target_pairs={{0,1},{1,2},{2,3},{3,4},{4,5},{5,6},{6,7},{7,8},{8,9},{9,10},{10,1... | collective-permute-start | bytes 196616 | tf_op jit(solution)/shard_map/while/body/eval_jaxpr/ppermute | solution.py:16
  352.8 17.0 %collective-permute-start = (bf16[128,512]{0,1:T(8,128)(2,1)S(1)}, bf16[128,512]{0,1:T(8,128)(2,1)S(1)}, u32[]{:S(2)}, u32[]{:S(2)}) collective-permute-start(bf16[128,512]{0,1:T(8,128)(2,1)S(1)} %get-tuple-element.555), channel_id=1, source_target_pairs={{1,0},{2,1},{3,2},{4,3},{5,4},{6,5},{7,6},{8,7},{9,8},{10,9},{11,1... | collective-permute-start | bytes 393224 | tf_op jit(solution)/shard_map/while/body/eval_jaxpr/ppermute | solution.py:16
  354.8 14.5 %collective-permute-start.1 = (bf16[64,512]{1,0:T(8,128)(2,1)S(1)}, bf16[64,512]{1,0:T(8,128)(2,1)S(1)}, u32[]{:S(2)}, u32[]{:S(2)}) collective-permute-start(bf16[64,512]{1,0:T(8,128)(2,1)S(1)} %get-tuple-element.554), channel_id=1, source_target_pairs={{0,1},{1,2},{2,3},{3,4},{4,5},{5,6},{6,7},{7,8},{8,9},{9,10},{10,1... | collective-permute-start | bytes 196616 | tf_op jit(solution)/shard_map/while/body/eval_jaxpr/ppermute | solution.py:16
  371.1 17.1 %collective-permute-start = (bf16[128,512]{0,1:T(8,128)(2,1)S(1)}, bf16[128,512]{0,1:T(8,128)(2,1)S(1)}, u32[]{:S(2)}, u32[]{:S(2)}) collective-permute-start(bf16[128,512]{0,1:T(8,128)(2,1)S(1)} %get-tuple-element.555), channel_id=1, source_target_pairs={{1,0},{2,1},{3,2},{4,3},{5,4},{6,5},{7,6},{8,7},{9,8},{10,9},{11,1... | collective-permute-start | bytes 393224 | tf_op jit(solution)/shard_map/while/body/eval_jaxpr/ppermute | solution.py:16
  (10 other events, 205.1 us)
Sparse Core Ops, SparseCore 0:
  9.4 72.8 all-gather.1
where the time goes:
time: 398 us; the launch traced here: 397 us
  waiting for transfers between devices  234 us (59%)
  starting transfers between devices  99.3 us (25%)
  matrix products  23.8 us (6%)
  other arithmetic  17 us (4%)
  between operations  14.2 us (4%)
  local copies, waits for them, and re-layouts  6.37 us (2%)
    ppermute x32, waiting for transfers between devices, shifted(): lax.ppermute(value, axis, [(source, source + steps) for source in range(i...  164 us
    ppermute x32, starting transfers between devices, shifted(): lax.ppermute(value, axis, [(source, source + steps) for source in range(i...  99.3 us
    all_gather x1, waiting for transfers between devices, body(): lax.all_gather(qkv_weight, 'seq', axis=1, tiled=True)  69.8 us
    dot_general x33, matrix products, absorb_block(): jnp.einsum('qhgd,khd->hgqk', query_head_rows, key_head_rows, preferred_el...  9.85 us
    dot_general x33, matrix products, absorb_block(): jnp.einsum('hgqk,khd->hgqd', weights.astype(jnp.bfloat16), value_head_row...  8.93 us
  transfers between devices with their start and end apart: 33, of which 17 were waited for; matrix products, arithmetic and copies ran while one was open for 5% of the time, Pallas kernels for 0%

commit v1 on v0

--- a/solution.py
+++ b/solution.py
@@ -47,7 +47,9 @@
     token_count = rows.shape[0]
     query_key_value = jnp.dot(
         rows,
-        lax.all_gather(qkv_weight, "seq", axis=1, tiled=True),
+        jnp.concatenate(
+            lax.all_to_all(jnp.stack([qkv_weight] * lax.axis_size("seq")), "seq", 0, 0), axis=1
+        ),
         preferred_element_type=jnp.float32,
     ).astype(jnp.bfloat16)
     lengths_row = doc_lengths[0]

time: 398 us -> 451 us (1.13)
  waiting for transfers between devices: 234 us -> 294 us
  between operations: 14.2 us -> 0.81 us
    all_to_all x0 -> x1, waiting for transfers between devices: none -> 134 us  [body(): lax.all_to_all(jnp.stack([qkv_weight] * lax.axis_size('seq')), 'seq', 0, 0)]
    all_gather x1 -> x0, waiting for transfers between devices: 69.8 us -> none  [body(): lax.all_gather(qkv_weight, 'seq', axis=1, tiled=True)]
    all_to_all x0 -> x1, starting transfers between devices: none -> 5.31 us  [body(): lax.all_to_all(jnp.stack([qkv_weight] * lax.axis_size('seq')), 'seq', 0, 0)]
  transfers between devices with their start and end apart: 33 -> 33, of which waited for: 17 -> 17; matrix products, arithmetic and copies ran while one was open for 5% -> 4% of each run, Pallas kernels for 0% -> 0%
where the time goes in v1:
time: 451 us; the launch traced here: 448 us
  waiting for transfers between devices  294 us (65%)
  starting transfers between devices  101 us (22%)
  matrix products  23.8 us (5%)
  other arithmetic  15.1 us (3%)
  local copies, waits for them, and re-layouts  10.4 us (2%)
    ppermute x32, waiting for transfers between devices, shifted(): lax.ppermute(value, axis, [(source, source + steps) for source in range(i...  160 us
    all_to_all x1, waiting for transfers between devices, body(): lax.all_to_all(jnp.stack([qkv_weight] * lax.axis_size('seq')), 'seq', 0, 0)  134 us
    ppermute x32, starting transfers between devices, shifted(): lax.ppermute(value, axis, [(source, source + steps) for source in range(i...  96.2 us
    dot_general x33, matrix products, absorb_block(): jnp.einsum('qhgd,khd->hgqk', query_head_rows, key_head_rows, preferred_el...  9.83 us
  transfers between devices with their start and end apart: 33, of which 17 were waited for; matrix products, arithmetic and copies ran while one was open for 4% of the time, Pallas kernels for 0%

profile of v1, /device:TPU:448, one launch (start us, length us, event | category | flops | bytes accessed | tf_op | source)
XLA Modules:
  0.0 448.2 jit_solution(392800579322837485)
XLA Ops:
  0.0 4.6 %stack.2 = bf16[8,2048,192]{1,2,0:T(8,128)(2,1)} broadcast(bf16[2048,192]{0,1:T(8,128)(2,1)} %param.7), dimensions={1,2} | broadcast | bytes 7077888 | tf_op jit(solution)/shard_map/stack | solution.py:51
  4.7 5.3 %all-to-all-start = ((bf16[8,2048,192]{1,2,0:T(8,128)(2,1)}), bf16[8,2048,192]{1,2,0:T(8,128)(2,1)}, u32[]{:S(2)}, u32[]{:S(2)}) async-start(bf16[8,2048,192]{1,2,0:T(8,128)(2,1)} %stack.2), calls=%async_computation | async-start | bytes 12582912 | tf_op jit(solution)/shard_map/all_to_all | solution.py:51
  12.6 133.8 %all-to-all-done = bf16[8,2048,192]{1,2,0:T(8,128)(2,1)} async-done(((bf16[8,2048,192]{1,2,0:T(8,128)(2,1)}), bf16[8,2048,192]{1,2,0:T(8,128)(2,1)}, u32[]{:S(2)}, u32[]{:S(2)}) %all-to-all-start) | async-done | bytes 6291488 | tf_op jit(solution)/shard_map/all_to_all | solution.py:51
  146.4 5.0 %convolution_convert_fusion = bf16[128,1536]{1,0:T(8,128)(2,1)S(1)} fusion(bf16[2048,1536]{0,1:T(8,128)(2,1)} %bitcast.4, bf16[1,128,2048]{2,1,0:T(8,128)(2,1)S(1)} %copy-done), kind=kOutput, calls=%fused_computation.36 | convolution fusion | flops 805502976 | bytes 7208960 | tf_op jit(solution)/shard_map/dot_general | solution.py:48
  153.3 294.0 %while.25 = (s32[]{:T(128)}, f32[4,4,128]{2,1,0:T(4,128)S(1)}, f32[4,4,128]{2,1,0:T(4,128)S(1)}, f32[4,4,128,64]{2,3,1,0:T(8,128)S(1)}, bf16[64,512]{1,0:T(8,128...) while((s32[]{:T(128)}, f32[4,4,128]{2,1,0:T(4,128)S(1)}, ...), condition=%wide.region_12.13_spmd.clone.clone, body=%wide.region_5.12_spmd.clone.clone.sunk | while | flops 104853896 | bytes 9559397 | solution.py:149
  153.3 6.6 %collective-permute-start = (bf16[128,512]{0,1:T(8,128)(2,1)S(1)}, bf16[128,512]{0,1:T(8,128)(2,1)S(1)}, u32[]{:S(2)}, u32[]{:S(2)}) collective-permute-start(bf16[128,512]{0,1:T(8,128)(2,1)S(1)} %get-tuple-element.555), channel_id=1, source_target_pairs={{1,0},{2,1},{3,2},{4,3},{5,4},{6,5},{7,6},{8,7},{9,8},{10,9},{11,1... | collective-permute-start | bytes 393224 | tf_op jit(solution)/shard_map/while/body/eval_jaxpr/ppermute | solution.py:16
  162.3 11.9 %collective-permute-done.1 = bf16[64,512]{1,0:T(8,128)(2,1)S(1)} collective-permute-done((bf16[64,512]{1,0:T(8,128)(2,1)S(1)}, bf16[64,512]{1,0:T(8,128)(2,1)S(1)}, u32[]{:S(2)}, u32[]{:S(2)}) %collective-permute-start.1) | collective-permute-done | bytes 65568 | tf_op jit(solution)/shard_map/while/body/eval_jaxpr/ppermute | solution.py:16
  177.9 3.9 collective-permute-start.1
  182.3 9.9 %collective-permute-done.1 = bf16[64,512]{1,0:T(8,128)(2,1)S(1)} collective-permute-done((bf16[64,512]{1,0:T(8,128)(2,1)S(1)}, bf16[64,512]{1,0:T(8,128)(2,1)S(1)}, u32[]{:S(2)}, u32[]{:S(2)}) %collective-permute-start.1) | collective-permute-done | bytes 65568 | tf_op jit(solution)/shard_map/while/body/eval_jaxpr/ppermute | solution.py:16
  200.4 9.9 %collective-permute-done.1 = bf16[64,512]{1,0:T(8,128)(2,1)S(1)} collective-permute-done((bf16[64,512]{1,0:T(8,128)(2,1)S(1)}, bf16[64,512]{1,0:T(8,128)(2,1)S(1)}, u32[]{:S(2)}, u32[]{:S(2)}) %collective-permute-start.1) | collective-permute-done | bytes 65568 | tf_op jit(solution)/shard_map/while/body/eval_jaxpr/ppermute | solution.py:16
  218.4 9.9 %collective-permute-done.1 = bf16[64,512]{1,0:T(8,128)(2,1)S(1)} collective-permute-done((bf16[64,512]{1,0:T(8,128)(2,1)S(1)}, bf16[64,512]{1,0:T(8,128)(2,1)S(1)}, u32[]{:S(2)}, u32[]{:S(2)}) %collective-permute-start.1) | collective-permute-done | bytes 65568 | tf_op jit(solution)/shard_map/while/body/eval_jaxpr/ppermute | solution.py:16
  232.0 3.9 collective-permute-start.1
  236.5 9.9 %collective-permute-done.1 = bf16[64,512]{1,0:T(8,128)(2,1)S(1)} collective-permute-done((bf16[64,512]{1,0:T(8,128)(2,1)S(1)}, bf16[64,512]{1,0:T(8,128)(2,1)S(1)}, u32[]{:S(2)}, u32[]{:S(2)}) %collective-permute-start.1) | collective-permute-done | bytes 65568 | tf_op jit(solution)/shard_map/while/body/eval_jaxpr/ppermute | solution.py:16
  254.5 9.9 %collective-permute-done.1 = bf16[64,512]{1,0:T(8,128)(2,1)S(1)} collective-permute-done((bf16[64,512]{1,0:T(8,128)(2,1)S(1)}, bf16[64,512]{1,0:T(8,128)(2,1)S(1)}, u32[]{:S(2)}, u32[]{:S(2)}) %collective-permute-start.1) | collective-permute-done | bytes 65568 | tf_op jit(solution)/shard_map/while/body/eval_jaxpr/ppermute | solution.py:16
  272.5 9.9 %collective-permute-done.1 = bf16[64,512]{1,0:T(8,128)(2,1)S(1)} collective-permute-done((bf16[64,512]{1,0:T(8,128)(2,1)S(1)}, bf16[64,512]{1,0:T(8,128)(2,1)S(1)}, u32[]{:S(2)}, u32[]{:S(2)}) %collective-permute-start.1) | collective-permute-done | bytes 65568 | tf_op jit(solution)/shard_map/while/body/eval_jaxpr/ppermute | solution.py:16
  290.6 9.9 %collective-permute-done.1 = bf16[64,512]{1,0:T(8,128)(2,1)S(1)} collective-permute-done((bf16[64,512]{1,0:T(8,128)(2,1)S(1)}, bf16[64,512]{1,0:T(8,128)(2,1)S(1)}, u32[]{:S(2)}, u32[]{:S(2)}) %collective-permute-start.1) | collective-permute-done | bytes 65568 | tf_op jit(solution)/shard_map/while/body/eval_jaxpr/ppermute | solution.py:16
  308.6 9.9 %collective-permute-done.1 = bf16[64,512]{1,0:T(8,128)(2,1)S(1)} collective-permute-done((bf16[64,512]{1,0:T(8,128)(2,1)S(1)}, bf16[64,512]{1,0:T(8,128)(2,1)S(1)}, u32[]{:S(2)}, u32[]{:S(2)}) %collective-permute-start.1) | collective-permute-done | bytes 65568 | tf_op jit(solution)/shard_map/while/body/eval_jaxpr/ppermute | solution.py:16
  326.7 9.9 %collective-permute-done.1 = bf16[64,512]{1,0:T(8,128)(2,1)S(1)} collective-permute-done((bf16[64,512]{1,0:T(8,128)(2,1)S(1)}, bf16[64,512]{1,0:T(8,128)(2,1)S(1)}, u32[]{:S(2)}, u32[]{:S(2)}) %collective-permute-start.1) | collective-permute-done | bytes 65568 | tf_op jit(solution)/shard_map/while/body/eval_jaxpr/ppermute | solution.py:16
  344.7 9.9 %collective-permute-done.1 = bf16[64,512]{1,0:T(8,128)(2,1)S(1)} collective-permute-done((bf16[64,512]{1,0:T(8,128)(2,1)S(1)}, bf16[64,512]{1,0:T(8,128)(2,1)S(1)}, u32[]{:S(2)}, u32[]{:S(2)}) %collective-permute-start.1) | collective-permute-done | bytes 65568 | tf_op jit(solution)/shard_map/while/body/eval_jaxpr/ppermute | solution.py:16
  362.7 10.3 %collective-permute-done.1 = bf16[64,512]{1,0:T(8,128)(2,1)S(1)} collective-permute-done((bf16[64,512]{1,0:T(8,128)(2,1)S(1)}, bf16[64,512]{1,0:T(8,128)(2,1)S(1)}, u32[]{:S(2)}, u32[]{:S(2)}) %collective-permute-start.1) | collective-permute-done | bytes 65568 | tf_op jit(solution)/shard_map/while/body/eval_jaxpr/ppermute | solution.py:16
  381.2 9.9 %collective-permute-done.1 = bf16[64,512]{1,0:T(8,128)(2,1)S(1)} collective-permute-done((bf16[64,512]{1,0:T(8,128)(2,1)S(1)}, bf16[64,512]{1,0:T(8,128)(2,1)S(1)}, u32[]{:S(2)}, u32[]{:S(2)}) %collective-permute-start.1) | collective-permute-done | bytes 65568 | tf_op jit(solution)/shard_map/while/body/eval_jaxpr/ppermute | solution.py:16
  399.3 10.0 %collective-permute-done.1 = bf16[64,512]{1,0:T(8,128)(2,1)S(1)} collective-permute-done((bf16[64,512]{1,0:T(8,128)(2,1)S(1)}, bf16[64,512]{1,0:T(8,128)(2,1)S(1)}, u32[]{:S(2)}, u32[]{:S(2)}) %collective-permute-start.1) | collective-permute-done | bytes 65568 | tf_op jit(solution)/shard_map/while/body/eval_jaxpr/ppermute | solution.py:16
  417.4 10.0 %collective-permute-done.1 = bf16[64,512]{1,0:T(8,128)(2,1)S(1)} collective-permute-done((bf16[64,512]{1,0:T(8,128)(2,1)S(1)}, bf16[64,512]{1,0:T(8,128)(2,1)S(1)}, u32[]{:S(2)}, u32[]{:S(2)}) %collective-permute-start.1) | collective-permute-done | bytes 65568 | tf_op jit(solution)/shard_map/while/body/eval_jaxpr/ppermute | solution.py:16
  435.6 9.9 %collective-permute-done.1 = bf16[64,512]{1,0:T(8,128)(2,1)S(1)} collective-permute-done((bf16[64,512]{1,0:T(8,128)(2,1)S(1)}, bf16[64,512]{1,0:T(8,128)(2,1)S(1)}, u32[]{:S(2)}, u32[]{:S(2)}) %collective-permute-start.1) | collective-permute-done | bytes 65568 | tf_op jit(solution)/shard_map/while/body/eval_jaxpr/ppermute | solution.py:16
  (437 shorter events, 121.3 us)
Async XLA Ops:
  4.7 141.8 %all-to-all-start = ((bf16[8,2048,192]{1,2,0:T(8,128)(2,1)}), bf16[8,2048,192]{1,2,0:T(8,128)(2,1)}, u32[]{:S(2)}, u32[]{:S(2)}) async-start(bf16[8,2048,192]{1,2,0:T(8,128)(2,1)} %stack.2), calls=%async_computation | async-start | bytes 12582912 | tf_op jit(solution)/shard_map/all_to_all | solution.py:51
  153.3 21.4 %collective-permute-start = (bf16[128,512]{0,1:T(8,128)(2,1)S(1)}, bf16[128,512]{0,1:T(8,128)(2,1)S(1)}, u32[]{:S(2)}, u32[]{:S(2)}) collective-permute-start(bf16[128,512]{0,1:T(8,128)(2,1)S(1)} %get-tuple-element.555), channel_id=1, source_target_pairs={{1,0},{2,1},{3,2},{4,3},{5,4},{6,5},{7,6},{8,7},{9,8},{10,9},{11,1... | collective-permute-start | bytes 393224 | tf_op jit(solution)/shard_map/while/body/eval_jaxpr/ppermute | solution.py:16
  176.0 16.7 %collective-permute-start = (bf16[128,512]{0,1:T(8,128)(2,1)S(1)}, bf16[128,512]{0,1:T(8,128)(2,1)S(1)}, u32[]{:S(2)}, u32[]{:S(2)}) collective-permute-start(bf16[128,512]{0,1:T(8,128)(2,1)S(1)} %get-tuple-element.555), channel_id=1, source_target_pairs={{1,0},{2,1},{3,2},{4,3},{5,4},{6,5},{7,6},{8,7},{9,8},{10,9},{11,1... | collective-permute-start | bytes 393224 | tf_op jit(solution)/shard_map/while/body/eval_jaxpr/ppermute | solution.py:16
  177.9 14.3 %collective-permute-start.1 = (bf16[64,512]{1,0:T(8,128)(2,1)S(1)}, bf16[64,512]{1,0:T(8,128)(2,1)S(1)}, u32[]{:S(2)}, u32[]{:S(2)}) collective-permute-start(bf16[64,512]{1,0:T(8,128)(2,1)S(1)} %get-tuple-element.554), channel_id=1, source_target_pairs={{0,1},{1,2},{2,3},{3,4},{4,5},{5,6},{6,7},{7,8},{8,9},{9,10},{10,1... | collective-permute-start | bytes 196616 | tf_op jit(solution)/shard_map/while/body/eval_jaxpr/ppermute | solution.py:16
  194.0 16.7 %collective-permute-start = (bf16[128,512]{0,1:T(8,128)(2,1)S(1)}, bf16[128,512]{0,1:T(8,128)(2,1)S(1)}, u32[]{:S(2)}, u32[]{:S(2)}) collective-permute-start(bf16[128,512]{0,1:T(8,128)(2,1)S(1)} %get-tuple-element.555), channel_id=1, source_target_pairs={{1,0},{2,1},{3,2},{4,3},{5,4},{6,5},{7,6},{8,7},{9,8},{10,9},{11,1... | collective-permute-start | bytes 393224 | tf_op jit(solution)/shard_map/while/body/eval_jaxpr/ppermute | solution.py:16
  212.1 16.7 %collective-permute-start = (bf16[128,512]{0,1:T(8,128)(2,1)S(1)}, bf16[128,512]{0,1:T(8,128)(2,1)S(1)}, u32[]{:S(2)}, u32[]{:S(2)}) collective-permute-start(bf16[128,512]{0,1:T(8,128)(2,1)S(1)} %get-tuple-element.555), channel_id=1, source_target_pairs={{1,0},{2,1},{3,2},{4,3},{5,4},{6,5},{7,6},{8,7},{9,8},{10,9},{11,1... | collective-permute-start | bytes 393224 | tf_op jit(solution)/shard_map/while/body/eval_jaxpr/ppermute | solution.py:16
  230.1 16.7 %collective-permute-start = (bf16[128,512]{0,1:T(8,128)(2,1)S(1)}, bf16[128,512]{0,1:T(8,128)(2,1)S(1)}, u32[]{:S(2)}, u32[]{:S(2)}) collective-permute-start(bf16[128,512]{0,1:T(8,128)(2,1)S(1)} %get-tuple-element.555), channel_id=1, source_target_pairs={{1,0},{2,1},{3,2},{4,3},{5,4},{6,5},{7,6},{8,7},{9,8},{10,9},{11,1... | collective-permute-start | bytes 393224 | tf_op jit(solution)/shard_map/while/body/eval_jaxpr/ppermute | solution.py:16
  232.0 14.3 %collective-permute-start.1 = (bf16[64,512]{1,0:T(8,128)(2,1)S(1)}, bf16[64,512]{1,0:T(8,128)(2,1)S(1)}, u32[]{:S(2)}, u32[]{:S(2)}) collective-permute-start(bf16[64,512]{1,0:T(8,128)(2,1)S(1)} %get-tuple-element.554), channel_id=1, source_target_pairs={{0,1},{1,2},{2,3},{3,4},{4,5},{5,6},{6,7},{7,8},{8,9},{9,10},{10,1... | collective-permute-start | bytes 196616 | tf_op jit(solution)/shard_map/while/body/eval_jaxpr/ppermute | solution.py:16
  248.1 16.7 %collective-permute-start = (bf16[128,512]{0,1:T(8,128)(2,1)S(1)}, bf16[128,512]{0,1:T(8,128)(2,1)S(1)}, u32[]{:S(2)}, u32[]{:S(2)}) collective-permute-start(bf16[128,512]{0,1:T(8,128)(2,1)S(1)} %get-tuple-element.555), channel_id=1, source_target_pairs={{1,0},{2,1},{3,2},{4,3},{5,4},{6,5},{7,6},{8,7},{9,8},{10,9},{11,1... | collective-permute-start | bytes 393224 | tf_op jit(solution)/shard_map/while/body/eval_jaxpr/ppermute | solution.py:16
  250.1 14.3 %collective-permute-start.1 = (bf16[64,512]{1,0:T(8,128)(2,1)S(1)}, bf16[64,512]{1,0:T(8,128)(2,1)S(1)}, u32[]{:S(2)}, u32[]{:S(2)}) collective-permute-start(bf16[64,512]{1,0:T(8,128)(2,1)S(1)} %get-tuple-element.554), channel_id=1, source_target_pairs={{0,1},{1,2},{2,3},{3,4},{4,5},{5,6},{6,7},{7,8},{8,9},{9,10},{10,1... | collective-permute-start | bytes 196616 | tf_op jit(solution)/shard_map/while/body/eval_jaxpr/ppermute | solution.py:16
  266.2 16.7 %collective-permute-start = (bf16[128,512]{0,1:T(8,128)(2,1)S(1)}, bf16[128,512]{0,1:T(8,128)(2,1)S(1)}, u32[]{:S(2)}, u32[]{:S(2)}) collective-permute-start(bf16[128,512]{0,1:T(8,128)(2,1)S(1)} %get-tuple-element.555), channel_id=1, source_target_pairs={{1,0},{2,1},{3,2},{4,3},{5,4},{6,5},{7,6},{8,7},{9,8},{10,9},{11,1... | collective-permute-start | bytes 393224 | tf_op jit(solution)/shard_map/while/body/eval_jaxpr/ppermute | solution.py:16
  268.1 14.3 %collective-permute-start.1 = (bf16[64,512]{1,0:T(8,128)(2,1)S(1)}, bf16[64,512]{1,0:T(8,128)(2,1)S(1)}, u32[]{:S(2)}, u32[]{:S(2)}) collective-permute-start(bf16[64,512]{1,0:T(8,128)(2,1)S(1)} %get-tuple-element.554), channel_id=1, source_target_pairs={{0,1},{1,2},{2,3},{3,4},{4,5},{5,6},{6,7},{7,8},{8,9},{9,10},{10,1... | collective-permute-start | bytes 196616 | tf_op jit(solution)/shard_map/while/body/eval_jaxpr/ppermute | solution.py:16
  284.2 16.7 %collective-permute-start = (bf16[128,512]{0,1:T(8,128)(2,1)S(1)}, bf16[128,512]{0,1:T(8,128)(2,1)S(1)}, u32[]{:S(2)}, u32[]{:S(2)}) collective-permute-start(bf16[128,512]{0,1:T(8,128)(2,1)S(1)} %get-tuple-element.555), channel_id=1, source_target_pairs={{1,0},{2,1},{3,2},{4,3},{5,4},{6,5},{7,6},{8,7},{9,8},{10,9},{11,1... | collective-permute-start | bytes 393224 | tf_op jit(solution)/shard_map/while/body/eval_jaxpr/ppermute | solution.py:16
  302.3 16.7 %collective-permute-start = (bf16[128,512]{0,1:T(8,128)(2,1)S(1)}, bf16[128,512]{0,1:T(8,128)(2,1)S(1)}, u32[]{:S(2)}, u32[]{:S(2)}) collective-permute-start(bf16[128,512]{0,1:T(8,128)(2,1)S(1)} %get-tuple-element.555), channel_id=1, source_target_pairs={{1,0},{2,1},{3,2},{4,3},{5,4},{6,5},{7,6},{8,7},{9,8},{10,9},{11,1... | collective-permute-start | bytes 393224 | tf_op jit(solution)/shard_map/while/body/eval_jaxpr/ppermute | solution.py:16
  320.3 16.7 %collective-permute-start = (bf16[128,512]{0,1:T(8,128)(2,1)S(1)}, bf16[128,512]{0,1:T(8,128)(2,1)S(1)}, u32[]{:S(2)}, u32[]{:S(2)}) collective-permute-start(bf16[128,512]{0,1:T(8,128)(2,1)S(1)} %get-tuple-element.555), channel_id=1, source_target_pairs={{1,0},{2,1},{3,2},{4,3},{5,4},{6,5},{7,6},{8,7},{9,8},{10,9},{11,1... | collective-permute-start | bytes 393224 | tf_op jit(solution)/shard_map/while/body/eval_jaxpr/ppermute | solution.py:16
  338.3 16.7 %collective-permute-start = (bf16[128,512]{0,1:T(8,128)(2,1)S(1)}, bf16[128,512]{0,1:T(8,128)(2,1)S(1)}, u32[]{:S(2)}, u32[]{:S(2)}) collective-permute-start(bf16[128,512]{0,1:T(8,128)(2,1)S(1)} %get-tuple-element.555), channel_id=1, source_target_pairs={{1,0},{2,1},{3,2},{4,3},{5,4},{6,5},{7,6},{8,7},{9,8},{10,9},{11,1... | collective-permute-start | bytes 393224 | tf_op jit(solution)/shard_map/while/body/eval_jaxpr/ppermute | solution.py:16
  356.4 17.1 %collective-permute-start = (bf16[128,512]{0,1:T(8,128)(2,1)S(1)}, bf16[128,512]{0,1:T(8,128)(2,1)S(1)}, u32[]{:S(2)}, u32[]{:S(2)}) collective-permute-start(bf16[128,512]{0,1:T(8,128)(2,1)S(1)} %get-tuple-element.555), channel_id=1, source_target_pairs={{1,0},{2,1},{3,2},{4,3},{5,4},{6,5},{7,6},{8,7},{9,8},{10,9},{11,1... | collective-permute-start | bytes 393224 | tf_op jit(solution)/shard_map/while/body/eval_jaxpr/ppermute | solution.py:16
  358.3 14.7 %collective-permute-start.1 = (bf16[64,512]{1,0:T(8,128)(2,1)S(1)}, bf16[64,512]{1,0:T(8,128)(2,1)S(1)}, u32[]{:S(2)}, u32[]{:S(2)}) collective-permute-start(bf16[64,512]{1,0:T(8,128)(2,1)S(1)} %get-tuple-element.554), channel_id=1, source_target_pairs={{0,1},{1,2},{2,3},{3,4},{4,5},{5,6},{6,7},{7,8},{8,9},{9,10},{10,1... | collective-permute-start | bytes 196616 | tf_op jit(solution)/shard_map/while/body/eval_jaxpr/ppermute | solution.py:16
  374.9 16.7 %collective-permute-start = (bf16[128,512]{0,1:T(8,128)(2,1)S(1)}, bf16[128,512]{0,1:T(8,128)(2,1)S(1)}, u32[]{:S(2)}, u32[]{:S(2)}) collective-permute-start(bf16[128,512]{0,1:T(8,128)(2,1)S(1)} %get-tuple-element.555), channel_id=1, source_target_pairs={{1,0},{2,1},{3,2},{4,3},{5,4},{6,5},{7,6},{8,7},{9,8},{10,9},{11,1... | collective-permute-start | bytes 393224 | tf_op jit(solution)/shard_map/while/body/eval_jaxpr/ppermute | solution.py:16
  392.9 16.8 %collective-permute-start = (bf16[128,512]{0,1:T(8,128)(2,1)S(1)}, bf16[128,512]{0,1:T(8,128)(2,1)S(1)}, u32[]{:S(2)}, u32[]{:S(2)}) collective-permute-start(bf16[128,512]{0,1:T(8,128)(2,1)S(1)} %get-tuple-element.555), channel_id=1, source_target_pairs={{1,0},{2,1},{3,2},{4,3},{5,4},{6,5},{7,6},{8,7},{9,8},{10,9},{11,1... | collective-permute-start | bytes 393224 | tf_op jit(solution)/shard_map/while/body/eval_jaxpr/ppermute | solution.py:16
  394.8 14.4 %collective-permute-start.1 = (bf16[64,512]{1,0:T(8,128)(2,1)S(1)}, bf16[64,512]{1,0:T(8,128)(2,1)S(1)}, u32[]{:S(2)}, u32[]{:S(2)}) collective-permute-start(bf16[64,512]{1,0:T(8,128)(2,1)S(1)} %get-tuple-element.554), channel_id=1, source_target_pairs={{0,1},{1,2},{2,3},{3,4},{4,5},{5,6},{6,7},{7,8},{8,9},{9,10},{10,1... | collective-permute-start | bytes 196616 | tf_op jit(solution)/shard_map/while/body/eval_jaxpr/ppermute | solution.py:16
  411.0 16.8 %collective-permute-start = (bf16[128,512]{0,1:T(8,128)(2,1)S(1)}, bf16[128,512]{0,1:T(8,128)(2,1)S(1)}, u32[]{:S(2)}, u32[]{:S(2)}) collective-permute-start(bf16[128,512]{0,1:T(8,128)(2,1)S(1)} %get-tuple-element.555), channel_id=1, source_target_pairs={{1,0},{2,1},{3,2},{4,3},{5,4},{6,5},{7,6},{8,7},{9,8},{10,9},{11,1... | collective-permute-start | bytes 393224 | tf_op jit(solution)/shard_map/while/body/eval_jaxpr/ppermute | solution.py:16
  413.0 14.4 %collective-permute-start.1 = (bf16[64,512]{1,0:T(8,128)(2,1)S(1)}, bf16[64,512]{1,0:T(8,128)(2,1)S(1)}, u32[]{:S(2)}, u32[]{:S(2)}) collective-permute-start(bf16[64,512]{1,0:T(8,128)(2,1)S(1)} %get-tuple-element.554), channel_id=1, source_target_pairs={{0,1},{1,2},{2,3},{3,4},{4,5},{5,6},{6,7},{7,8},{8,9},{9,10},{10,1... | collective-permute-start | bytes 196616 | tf_op jit(solution)/shard_map/while/body/eval_jaxpr/ppermute | solution.py:16
  429.2 16.7 %collective-permute-start = (bf16[128,512]{0,1:T(8,128)(2,1)S(1)}, bf16[128,512]{0,1:T(8,128)(2,1)S(1)}, u32[]{:S(2)}, u32[]{:S(2)}) collective-permute-start(bf16[128,512]{0,1:T(8,128)(2,1)S(1)} %get-tuple-element.555), channel_id=1, source_target_pairs={{1,0},{2,1},{3,2},{4,3},{5,4},{6,5},{7,6},{8,7},{9,8},{10,9},{11,1... | collective-permute-start | bytes 393224 | tf_op jit(solution)/shard_map/while/body/eval_jaxpr/ppermute | solution.py:16
  (12 other events, 285.8 us)
